TPU v7x, 512 devices: a whole 4x4x16 slice. The times are simulated.
512 devices in a mesh: gx: 32 (over z_hi, x, core), gy: 16 (over y, z_lo).
Axes of the slice: x: 4, y: 4, z: 16 (z_hi: 4, z_lo: 4; z = z_hi * 4 + z_lo), core: 2. Of those that a mesh axis runs over, the one named last changes fastest.
Arguments:
- orbitals: float32 [32, 64, 128, 512], P(None, 'gx', 'gy'), may hold values from -60 to 60
- potential: float32 [64, 128, 512], P('gx', 'gy'), may hold values from 0.2 to 2
- sign_bits: int32 [64, 128, 512], P('gx', 'gy'), may hold values from 0 to 1
- sampled_rows: int32 [32, 16, 8192], P('gx', 'gy'), may hold values from 0 to 8191, each once within a row
Outputs:
- rotated: float32 [32, 64, 128, 512], P(None, 'gx', 'gy')
- sketches: float32 [2, 32, 4096], P(None, None, ('gx', 'gy'))
- projected: float32 [32, 32], replicated
Inputs may be any that keep to these rules, and one draw needn't show every extreme that they name: Each block's row of sampled_rows holds every one of its 8192 cell numbers once.
All inputs are finite; a program needn't handle non-finite values.
Results may differ from a plain program's by a relative error of at most 0.00026.
Values sent between devices are 32-bit elements; how exact they have to be, the bound alone decides.
No kernel may reach another device: no remote copies, remote signals or barrier semaphores. Data moves between devices by JAX's collectives and lax.ppermute only.
A program may use at most 64 MiB of HBM per device.

v0:
```python
import jax
import jax.numpy as jnp
from jax import lax
from jax.sharding import PartitionSpec as P

M = 4096
HIGHEST = lax.Precision.HIGHEST
filter_center = 6.25
filter_half = 4.25


def padded_2(array, sides, width):
    for axis, dim in sides:
        size, length = (lax.axis_size(axis), array.shape[dim])
        up = [(i, (i + 1) % size) for i in range(size - 1)]
        down = [(j, i) for i, j in up]
        last = lax.slice_in_dim(array, length - width, length, axis=dim)
        initial = lax.slice_in_dim(array, 0, width, axis=dim)
        before = lax.ppermute(last, axis, up)
        after = lax.ppermute(initial, axis, down)
        array = jnp.concatenate([before, array, after], axis=dim)
    return array


def hadamard_table(order):
    index = jnp.arange(order, dtype=jnp.int32)
    parity = jnp.zeros((order, order), jnp.int32)
    for bit in range(order.bit_length() - 1):
        weight = 2**bit
        parity = parity + index[:, None] // weight % 2 * (index[None, :] // weight % 2)
    return (1 - 2 * (parity % 2)).astype(jnp.float32)


def second_diff(padded, axis, count):
    parts = [lax.slice_in_dim(padded, k, k + count, axis=axis) for k in range(5)]
    return (16.0 * (parts[1] + parts[3]) - (parts[0] + parts[4]) - 30.0 * parts[2]) / 12.0


def apply_ham(field, potential):
    padded = padded_2(field, (("gx", 1), ("gy", 2)), 2)
    x_padded = padded[:, :, 2:-2, :]
    y_padded = padded[:, 2:-2, :, :]
    z_padded = jnp.pad(field, ((0, 0), (0, 0), (0, 0), (2, 2)))
    total = second_diff(x_padded, 1, field.shape[1])
    total = total + second_diff(y_padded, 2, field.shape[2])
    total = total + second_diff(z_padded, 3, field.shape[3])
    return -0.5 * total + potential[None] * field


def shards(orbitals, potential, sign_bits, sampled_rows):
    first = (apply_ham(orbitals, potential) - filter_center * orbitals) / filter_half
    second = 2.0 * (apply_ham(first, potential) - filter_center * first) / filter_half - orbitals
    filtered = 2.0 * (apply_ham(second, potential) - filter_center * second) / filter_half - first
    applied = apply_ham(filtered, potential)
    count = orbitals.shape[0]
    cells = orbitals.shape[1] * orbitals.shape[2] * orbitals.shape[3]
    stacked = jnp.concatenate([filtered, applied], axis=0)
    sign_block = (2 * sign_bits - 1).astype(jnp.float32)
    flat = (stacked * sign_block[None]).reshape(2 * count, -1, 128)
    mixed = jnp.einsum("nac,cd->nad", flat, hadamard_table(128), precision=HIGHEST)
    mixed = jnp.einsum("ba,nac->nbc", hadamard_table(cells // 128), mixed, precision=HIGHEST)
    mixed = mixed.reshape(2 * count, cells)
    picked = jnp.take(mixed, sampled_rows[0, 0, :M], axis=1)
    devices = lax.axis_size("gx") * lax.axis_size("gy")
    term = (picked / jnp.sqrt(jnp.float32(M * devices))).reshape(2, count, M)
    width = M // devices
    total = lax.psum(term, ("gx", "gy"))
    position = lax.axis_index("gx") * lax.axis_size("gy") + lax.axis_index("gy")
    share = lax.dynamic_slice_in_dim(total, position * width, width, 2)
    gram = jnp.dot(total[0], total[0].T, precision=HIGHEST) / cells
    cross = jnp.dot(total[0], total[1].T, precision=HIGHEST) / cells
    lower = jnp.linalg.cholesky(gram)
    inverse = lax.linalg.triangular_solve(
        lower, jnp.eye(count, dtype=jnp.float32), left_side=True, lower=True
    )
    rotated = jnp.dot(inverse, filtered.reshape(count, -1), precision=HIGHEST).reshape(
        filtered.shape
    )
    inner = jnp.dot(jnp.dot(inverse, cross, precision=HIGHEST), inverse.T, precision=HIGHEST)
    projected = 0.5 * (inner + inner.T)
    return (rotated, share, projected)


def solution(mesh):
    in_specs = (
        P(None, "gx", "gy", None),
        P("gx", "gy", None),
        P("gx", "gy", None),
        P("gx", "gy", None),
    )
    out_specs = (P(None, "gx", "gy", None), P(None, None, ("gx", "gy")), P())
    return jax.shard_map(shards, mesh=mesh, in_specs=in_specs, out_specs=out_specs, check_vma=False)
```

profile of v0, /device:TPU:1, one launch (start us, length us, event | category | flops | bytes accessed | tf_op | source)
XLA Modules:
  0.0 938.2 jit_solution(11268816920238034277)
XLA Ops:
  9.1 4.5 collective-permute-start
  13.7 5.6 collective-permute-start.1
  19.3 6.1 collective-permute-done
  26.1 4.0 collective-permute-done.1
  30.3 3.6 collective-permute-start.2
  35.2 7.6 collective-permute-done.2
  42.8 28.2 %collective-permute-done.3 = f32[32,6,2,512]{3,0,2,1:T(8,128)S(1)} collective-permute-done((f32[32,6,2,512]{3,0,2,1:T(8,128)S(1)}, f32[32,6,2,512]{3,0,2,1:T(8,128)S(1)}, u32[]{:S(2)}, u32[]{:S(2)}) %collective-permute-start.3) | collective-permute-done | bytes 786464 | tf_op jit(solution)/shard_map/ppermute | solution.py:20
  77.3 9.8 %collective-permute-done.4 = f32[32,2,8,512]{3,0,2,1:T(8,128)S(1)} collective-permute-done((f32[32,2,8,512]{3,0,2,1:T(8,128)S(1)}, f32[32,2,8,512]{3,0,2,1:T(8,128)S(1)}, u32[]{:S(2)}, u32[]{:S(2)}) %collective-permute-start.4) | collective-permute-done | bytes 1048608 | tf_op jit(solution)/shard_map/ppermute | solution.py:19
  87.1 4.4 collective-permute-done.5
  91.6 7.8 collective-permute-start.6
  100.7 7.6 collective-permute-done.6
  108.2 26.3 %collective-permute-done.7 = f32[32,6,2,512]{3,0,2,1:T(8,128)S(1)} collective-permute-done((f32[32,6,2,512]{3,0,2,1:T(8,128)S(1)}, f32[32,6,2,512]{3,0,2,1:T(8,128)S(1)}, u32[]{:S(2)}, u32[]{:S(2)}) %collective-permute-start.7) | collective-permute-done | bytes 786464 | tf_op jit(solution)/shard_map/ppermute | solution.py:20
  141.3 9.2 collective-permute-done.8
  150.6 4.4 collective-permute-done.9
  159.5 7.5 collective-permute-done.10
  167.0 24.4 %collective-permute-done.11 = f32[32,6,2,512]{3,0,2,1:T(8,128)S(1)} collective-permute-done((f32[32,6,2,512]{3,0,2,1:T(8,128)S(1)}, f32[32,6,2,512]{3,0,2,1:T(8,128)S(1)}, u32[]{:S(2)}, u32[]{:S(2)}) %collective-permute-start.11) | collective-permute-done | bytes 786464 | tf_op jit(solution)/shard_map/ppermute | solution.py:20
  197.7 9.1 collective-permute-done.12
  206.8 22.0 %collective-permute-done.13 = f32[32,2,8,512]{3,0,2,1:T(8,128)S(1)} collective-permute-done((f32[32,2,8,512]{3,0,2,1:T(8,128)S(1)}, f32[32,2,8,512]{3,0,2,1:T(8,128)S(1)}, u32[]{:S(2)}, u32[]{:S(2)}) %collective-permute-start.13) | collective-permute-done | bytes 1048608 | tf_op jit(solution)/shard_map/ppermute | solution.py:20
  230.3 3.5 collective-permute-start.14
  235.7 6.3 collective-permute-done.14
  242.1 27.8 %collective-permute-done.15 = f32[32,6,2,512]{3,0,2,1:T(8,128)} collective-permute-done((f32[32,6,2,512]{3,0,2,1:T(8,128)}, f32[32,6,2,512]{3,0,2,1:T(8,128)}, u32[]{:S(2)}, u32[]{:S(2)}) %collective-permute-start.15) | collective-permute-done | bytes 786464 | tf_op jit(solution)/shard_map/ppermute | solution.py:20
  269.9 3.4 fusion.40
  282.9 13.0 %gather_fusion = f32[4096,64]{1,0:T(8,128)S(1)} fusion(f32[64,8192]{0,1:T(8,128)} %bitcast.60, s32[4096]{0:T(1024)S(1)} %broadcast_clamp_fusion), kind=kCustom, calls=%fused_computation | custom fusion | bytes 2113536 | tf_op jit(solution)/shard_map/jit(_take)/gather | solution.py:63
  300.4 614.8 %all-reduce.6.cloned.1.call-done = f32[2,32,4096]{2,1,0:T(8,128)} async-done(((f32[2,32,4096]{2,1,0:T(8,128)}), f32[2,32,4096]{2,1,0:T(8,128)}) %all-reduce.6.cloned.1.call-update) | async-done | bytes 1048592 | tf_op jit(solution)/shard_map/psum | solution.py:67
  (79 shorter events, 63.1 us)
Async XLA Ops:
  7.2 18.3 %copy-start = (f32[32,2,8,512]{3,2,1,0:T(8,128)S(1)}, f32[32,2,8,512]{3,2,1,0:T(8,128)}, u32[]{:S(2)}) copy-start(f32[32,2,8,512]{3,2,1,0:T(8,128)} %param.4) | copy-start | bytes 3145732
  7.2 908.0 %all-reduce.6.cloned.1.call-start = ((), (), s32[]{:S(2)}) async-start(), calls=%async_computation | async-start | bytes 2097152 | tf_op jit(solution)/shard_map/psum | solution.py:67
  9.1 16.2 %collective-permute-start = (f32[32,2,8,512]{3,0,2,1:T(8,128)S(1)}, f32[32,2,8,512]{3,0,2,1:T(8,128)S(1)}, u32[]{:S(2)}, u32[]{:S(2)}) collective-permute-start(f32[32,2,8,512]{3,0,2,1:T(8,128)S(1)} %copy.36), channel_id=1, source_target_pairs={{0,16},{16,32},{32,48},{48,64},{64,80},{80,96},{96,112},{112,128},... | collective-permute-start | bytes 3145736 | tf_op jit(solution)/shard_map/ppermute | solution.py:19
  13.7 16.4 %collective-permute-start.1 = (f32[32,2,8,512]{3,0,2,1:T(8,128)S(1)}, f32[32,2,8,512]{3,0,2,1:T(8,128)S(1)}, u32[]{:S(2)}, u32[]{:S(2)}) collective-permute-start(f32[32,2,8,512]{3,0,2,1:T(8,128)S(1)} %copy.36), channel_id=1, source_target_pairs={{16,0},{32,16},{48,32},{64,48},{80,64},{96,80},{112,96},{128,112},... | collective-permute-start | bytes 3145736 | tf_op jit(solution)/shard_map/ppermute | solution.py:20
  30.2 40.8 %copy-start.3 = (f32[2,8,512]{2,1,0:T(8,128)S(1)}, f32[2,8,512]{2,1,0:T(8,128)}, u32[]{:S(2)}) copy-start(f32[2,8,512]{2,1,0:T(8,128)} %param.5) | copy-start | bytes 98308
  30.3 12.5 %collective-permute-start.2 = (f32[32,6,2,512]{3,0,2,1:T(8,128)S(1)}, f32[32,6,2,512]{3,0,2,1:T(8,128)S(1)}, u32[]{:S(2)}, u32[]{:S(2)}) collective-permute-start(f32[32,6,2,512]{3,0,2,1:T(8,128)S(1)} %get-tuple-element.23), channel_id=1, source_target_pairs={{0,1},{1,2},{2,3},{3,4},{4,5},{5,6},{6,7},{7,8},{8,9},{9,10},{10,1... | collective-permute-start | bytes 2359304 | tf_op jit(solution)/shard_map/ppermute | solution.py:19
  33.9 37.1 %collective-permute-start.3 = (f32[32,6,2,512]{3,0,2,1:T(8,128)S(1)}, f32[32,6,2,512]{3,0,2,1:T(8,128)S(1)}, u32[]{:S(2)}, u32[]{:S(2)}) collective-permute-start(f32[32,6,2,512]{3,0,2,1:T(8,128)S(1)} %get-tuple-element.24), channel_id=1, source_target_pairs={{1,0},{2,1},{3,2},{4,3},{5,4},{6,5},{7,6},{8,7},{9,8},{10,9},{11,1... | collective-permute-start | bytes 2359304 | tf_op jit(solution)/shard_map/ppermute | solution.py:20
  72.6 14.4 %collective-permute-start.4 = (f32[32,2,8,512]{3,0,2,1:T(8,128)S(1)}, f32[32,2,8,512]{3,0,2,1:T(8,128)S(1)}, u32[]{:S(2)}, u32[]{:S(2)}) collective-permute-start(f32[32,2,8,512]{3,0,2,1:T(8,128)S(1)} %get-tuple-element.15), channel_id=1, source_target_pairs={{0,16},{16,32},{32,48},{48,64},{64,80},{80,96},{96,112},{112,128},... | collective-permute-start | bytes 3145736 | tf_op jit(solution)/shard_map/ppermute | solution.py:19
  75.3 16.1 %collective-permute-start.5 = (f32[32,2,8,512]{3,0,2,1:T(8,128)S(1)}, f32[32,2,8,512]{3,0,2,1:T(8,128)S(1)}, u32[]{:S(2)}, u32[]{:S(2)}) collective-permute-start(f32[32,2,8,512]{3,0,2,1:T(8,128)S(1)} %get-tuple-element.15), channel_id=1, source_target_pairs={{16,0},{32,16},{48,32},{64,48},{80,64},{96,80},{112,96},{128,112},... | collective-permute-start | bytes 3145736 | tf_op jit(solution)/shard_map/ppermute | solution.py:20
  91.6 16.7 %collective-permute-start.6 = (f32[32,6,2,512]{3,0,2,1:T(8,128)S(1)}, f32[32,6,2,512]{3,0,2,1:T(8,128)S(1)}, u32[]{:S(2)}, u32[]{:S(2)}) collective-permute-start(f32[32,6,2,512]{3,0,2,1:T(8,128)S(1)} %get-tuple-element.21), channel_id=1, source_target_pairs={{0,1},{1,2},{2,3},{3,4},{4,5},{5,6},{6,7},{7,8},{8,9},{9,10},{10,1... | collective-permute-start | bytes 2359304 | tf_op jit(solution)/shard_map/ppermute | solution.py:19
  99.4 35.2 %collective-permute-start.7 = (f32[32,6,2,512]{3,0,2,1:T(8,128)S(1)}, f32[32,6,2,512]{3,0,2,1:T(8,128)S(1)}, u32[]{:S(2)}, u32[]{:S(2)}) collective-permute-start(f32[32,6,2,512]{3,0,2,1:T(8,128)S(1)} %get-tuple-element.22), channel_id=1, source_target_pairs={{1,0},{2,1},{3,2},{4,3},{5,4},{6,5},{7,6},{8,7},{9,8},{10,9},{11,1... | collective-permute-start | bytes 2359304 | tf_op jit(solution)/shard_map/ppermute | solution.py:20
  136.9 13.7 %collective-permute-start.8 = (f32[32,2,8,512]{3,0,2,1:T(8,128)S(1)}, f32[32,2,8,512]{3,0,2,1:T(8,128)S(1)}, u32[]{:S(2)}, u32[]{:S(2)}) collective-permute-start(f32[32,2,8,512]{3,0,2,1:T(8,128)S(1)} %fusion.21), channel_id=1, source_target_pairs={{0,16},{16,32},{32,48},{48,64},{64,80},{80,96},{96,112},{112,128},... | collective-permute-start | bytes 3145736 | tf_op jit(solution)/shard_map/ppermute | solution.py:19
  138.9 16.1 %collective-permute-start.9 = (f32[32,2,8,512]{3,0,2,1:T(8,128)S(1)}, f32[32,2,8,512]{3,0,2,1:T(8,128)S(1)}, u32[]{:S(2)}, u32[]{:S(2)}) collective-permute-start(f32[32,2,8,512]{3,0,2,1:T(8,128)S(1)} %fusion.21), channel_id=1, source_target_pairs={{16,0},{32,16},{48,32},{64,48},{80,64},{96,80},{112,96},{128,112},... | collective-permute-start | bytes 3145736 | tf_op jit(solution)/shard_map/ppermute | solution.py:20
  155.1 11.9 %collective-permute-start.10 = (f32[32,6,2,512]{3,0,2,1:T(8,128)S(1)}, f32[32,6,2,512]{3,0,2,1:T(8,128)S(1)}, u32[]{:S(2)}, u32[]{:S(2)}) collective-permute-start(f32[32,6,2,512]{3,0,2,1:T(8,128)S(1)} %get-tuple-element.19), channel_id=1, source_target_pairs={{0,1},{1,2},{2,3},{3,4},{4,5},{5,6},{6,7},{7,8},{8,9},{9,10},{10,1... | collective-permute-start | bytes 2359304 | tf_op jit(solution)/shard_map/ppermute | solution.py:19
  158.1 39.4 %copy-start.5 = (s32[2,8,512]{2,1,0:T(8,128)S(1)}, s32[2,8,512]{2,1,0:T(8,128)}, u32[]{:S(2)}) copy-start(s32[2,8,512]{2,1,0:T(8,128)} %param.6) | copy-start | bytes 98308
  158.2 39.5 %slice-start = ((s32[1,1,8192]{2,1,0:T(1,128)}), s32[1,1,4096]{2,1,0:T(1,128)S(1)}, s32[]{:S(2)}) async-start(s32[1,1,8192]{2,1,0:T(1,128)} %param.7), calls=%async_computation.1 | async-start | bytes 32768 | tf_op jit(solution)/shard_map/slice | solution.py:63
  158.2 33.2 %collective-permute-start.11 = (f32[32,6,2,512]{3,0,2,1:T(8,128)S(1)}, f32[32,6,2,512]{3,0,2,1:T(8,128)S(1)}, u32[]{:S(2)}, u32[]{:S(2)}) collective-permute-start(f32[32,6,2,512]{3,0,2,1:T(8,128)S(1)} %get-tuple-element.20), channel_id=1, source_target_pairs={{1,0},{2,1},{3,2},{4,3},{5,4},{6,5},{7,6},{8,7},{9,8},{10,9},{11,1... | collective-permute-start | bytes 2359304 | tf_op jit(solution)/shard_map/ppermute | solution.py:20
  193.2 13.7 %collective-permute-start.12 = (f32[32,2,8,512]{3,0,2,1:T(8,128)S(1)}, f32[32,2,8,512]{3,0,2,1:T(8,128)S(1)}, u32[]{:S(2)}, u32[]{:S(2)}) collective-permute-start(f32[32,2,8,512]{3,0,2,1:T(8,128)S(1)} %fusion.32), channel_id=1, source_target_pairs={{0,16},{16,32},{32,48},{48,64},{64,80},{80,96},{96,112},{112,128},... | collective-permute-start | bytes 3145736 | tf_op jit(solution)/shard_map/ppermute | solution.py:19
  195.1 33.7 %collective-permute-start.13 = (f32[32,2,8,512]{3,0,2,1:T(8,128)S(1)}, f32[32,2,8,512]{3,0,2,1:T(8,128)S(1)}, u32[]{:S(2)}, u32[]{:S(2)}) collective-permute-start(f32[32,2,8,512]{3,0,2,1:T(8,128)S(1)} %fusion.32), channel_id=1, source_target_pairs={{16,0},{32,16},{48,32},{64,48},{80,64},{96,80},{112,96},{128,112},... | collective-permute-start | bytes 3145736 | tf_op jit(solution)/shard_map/ppermute | solution.py:20
  197.7 37.3 %copy-start.4 = (s32[1,1,8192]{2,1,0:T(1,128)S(1)}, s32[1,1,8192]{2,1,0:T(1,128)}, u32[]{:S(2)}) copy-start(s32[1,1,8192]{2,1,0:T(1,128)} %param.7) | copy-start | bytes 98308
  206.8 23.4 %copy-start.1 = (f32[32,2,8,512]{3,0,2,1:T(8,128)}, f32[32,2,8,512]{3,0,2,1:T(8,128)S(1)}, u32[]{:S(2)}) copy-start(f32[32,2,8,512]{3,0,2,1:T(8,128)S(1)} %collective-permute-done.12) | copy-start | bytes 3145732
  228.8 1.5 copy-start.2
  230.3 11.8 %collective-permute-start.14 = (f32[32,6,2,512]{3,0,2,1:T(8,128)}, f32[32,6,2,512]{3,0,2,1:T(8,128)}, u32[]{:S(2)}, u32[]{:S(2)}) collective-permute-start(f32[32,6,2,512]{3,0,2,1:T(8,128)} %get-tuple-element.17), channel_id=1, source_target_pairs={{0,1},{1,2},{2,3},{3,4},{4,5},{5,6},{6,7},{7,8},{8,9},{9,10},{10,1... | collective-permute-start | bytes 2359304 | tf_op jit(solution)/shard_map/ppermute | solution.py:19
  233.7 36.1 %collective-permute-start.15 = (f32[32,6,2,512]{3,0,2,1:T(8,128)}, f32[32,6,2,512]{3,0,2,1:T(8,128)}, u32[]{:S(2)}, u32[]{:S(2)}) collective-permute-start(f32[32,6,2,512]{3,0,2,1:T(8,128)} %get-tuple-element.18), channel_id=1, source_target_pairs={{1,0},{2,1},{3,2},{4,3},{5,4},{6,5},{7,6},{8,7},{9,8},{10,9},{11,1... | collective-permute-start | bytes 2359304 | tf_op jit(solution)/shard_map/ppermute | solution.py:20
Sparse Core Ops, SparseCore 0:
  299.9 615.2 all-reduce.5
where the time goes:
time: 939 us; the launch traced here: 938 us
  waiting for transfers between devices  819 us (87%)
  starting transfers between devices  46.6 us (5%)
  local copies, waits for them, and re-layouts  27.6 us (3%)
  other arithmetic  20.5 us (2%)
  between operations  14.5 us (2%)
  matrix products  9.67 us (1%)
    psum x1, waiting for transfers between devices, shards(): total = lax.psum(term, ('gx', 'gy'))  615 us
    ppermute x8, waiting for transfers between devices, padded_2(): after = lax.ppermute(initial, axis, down)  141 us
    ppermute x8, waiting for transfers between devices, padded_2(): before = lax.ppermute(last, axis, up)  63.2 us
    ppermute x8, starting transfers between devices, padded_2(): before = lax.ppermute(last, axis, up)  28.9 us
  transfers between devices with their start and end apart: 17, of which 17 were waited for; matrix products, arithmetic and copies ran while one was open for 0% of the time, Pallas kernels for 0%

commit v1 on v0

--- a/solution.py
+++ b/solution.py
@@ -64,7 +64,7 @@
     devices = lax.axis_size("gx") * lax.axis_size("gy")
     term = (picked / jnp.sqrt(jnp.float32(M * devices))).reshape(2, count, M)
     width = M // devices
-    total = lax.psum(term, ("gx", "gy"))
+    total = lax.psum(lax.psum(term, "gy"), "gx")
     position = lax.axis_index("gx") * lax.axis_size("gy") + lax.axis_index("gy")
     share = lax.dynamic_slice_in_dim(total, position * width, width, 2)
     gram = jnp.dot(total[0], total[0].T, precision=HIGHEST) / cells

time: 939 us -> 1000 us (1.065)
  waiting for transfers between devices: 819 us -> 880 us
    psum x1 -> x2, waiting for transfers between devices: 615 us -> 676 us  [shards(): total = lax.psum(lax.psum(term, 'gy'), 'gx')]
  transfers between devices with their start and end apart: 17 -> 18, of which waited for: 17 -> 18; matrix products, arithmetic and copies ran while one was open for 0% -> 0% of each run, Pallas kernels for 0% -> 0%
where the time goes in v1:
time: 1000 us; the launch traced here: 999 us
  waiting for transfers between devices  880 us (88%)
  starting transfers between devices  47 us (5%)
  local copies, waits for them, and re-layouts  27.6 us (3%)
  other arithmetic  20.3 us (2%)
  between operations  14.5 us (1%)
    psum x2, waiting for transfers between devices, shards(): total = lax.psum(lax.psum(term, 'gy'), 'gx')  676 us
    ppermute x8, waiting for transfers between devices, padded_2(): after = lax.ppermute(initial, axis, down)  141 us
    ppermute x8, waiting for transfers between devices, padded_2(): before = lax.ppermute(last, axis, up)  63 us
    ppermute x8, starting transfers between devices, padded_2(): before = lax.ppermute(last, axis, up)  28.9 us
  transfers between devices with their start and end apart: 18, of which 18 were waited for; matrix products, arithmetic and copies ran while one was open for 0% of the time, Pallas kernels for 0%

profile of v1, /device:TPU:1, one launch (start us, length us, event | category | flops | bytes accessed | tf_op | source)
XLA Modules:
  0.0 999.4 jit_solution(14002218086486717917)
XLA Ops:
  9.1 4.5 collective-permute-start
  13.7 5.6 collective-permute-start.1
  19.3 6.1 collective-permute-done
  26.1 4.0 collective-permute-done.1
  30.3 3.6 collective-permute-start.2
  35.2 7.6 collective-permute-done.2
  42.8 28.2 %collective-permute-done.3 = f32[32,6,2,512]{3,0,2,1:T(8,128)S(1)} collective-permute-done((f32[32,6,2,512]{3,0,2,1:T(8,128)S(1)}, f32[32,6,2,512]{3,0,2,1:T(8,128)S(1)}, u32[]{:S(2)}, u32[]{:S(2)}) %collective-permute-start.3) | collective-permute-done | bytes 786464 | tf_op jit(solution)/shard_map/ppermute | solution.py:20
  77.3 9.8 collective-permute-done.4
  87.1 4.4 collective-permute-done.5
  91.6 7.8 collective-permute-start.6
  100.7 7.6 collective-permute-done.6
  108.2 26.3 %collective-permute-done.7 = f32[32,6,2,512]{3,0,2,1:T(8,128)S(1)} collective-permute-done((f32[32,6,2,512]{3,0,2,1:T(8,128)S(1)}, f32[32,6,2,512]{3,0,2,1:T(8,128)S(1)}, u32[]{:S(2)}, u32[]{:S(2)}) %collective-permute-start.7) | collective-permute-done | bytes 786464 | tf_op jit(solution)/shard_map/ppermute | solution.py:20
  141.3 9.2 collective-permute-done.8
  150.6 4.4 collective-permute-done.9
  159.5 7.5 collective-permute-done.10
  167.0 24.4 %collective-permute-done.11 = f32[32,6,2,512]{3,0,2,1:T(8,128)S(1)} collective-permute-done((f32[32,6,2,512]{3,0,2,1:T(8,128)S(1)}, f32[32,6,2,512]{3,0,2,1:T(8,128)S(1)}, u32[]{:S(2)}, u32[]{:S(2)}) %collective-permute-start.11) | collective-permute-done | bytes 786464 | tf_op jit(solution)/shard_map/ppermute | solution.py:20
  197.7 9.1 collective-permute-done.12
  206.8 22.0 %collective-permute-done.13 = f32[32,2,8,512]{3,0,2,1:T(8,128)S(1)} collective-permute-done((f32[32,2,8,512]{3,0,2,1:T(8,128)S(1)}, f32[32,2,8,512]{3,0,2,1:T(8,128)S(1)}, u32[]{:S(2)}, u32[]{:S(2)}) %collective-permute-start.13) | collective-permute-done | bytes 1048608 | tf_op jit(solution)/shard_map/ppermute | solution.py:20
  230.3 3.5 collective-permute-start.14
  235.9 6.1 collective-permute-done.14
  242.1 27.8 %collective-permute-done.15 = f32[32,6,2,512]{3,0,2,1:T(8,128)} collective-permute-done((f32[32,6,2,512]{3,0,2,1:T(8,128)}, f32[32,6,2,512]{3,0,2,1:T(8,128)}, u32[]{:S(2)}, u32[]{:S(2)}) %collective-permute-start.15) | collective-permute-done | bytes 786464 | tf_op jit(solution)/shard_map/ppermute | solution.py:20
  282.8 13.0 %gather_fusion = f32[4096,64]{1,0:T(8,128)S(1)} fusion(f32[64,8192]{0,1:T(8,128)} %bitcast.60, s32[4096]{0:T(1024)S(1)} %broadcast_clamp_fusion), kind=kCustom, calls=%fused_computation | custom fusion | bytes 2113536 | tf_op jit(solution)/shard_map/jit(_take)/gather | solution.py:63
  299.9 313.4 %all-reduce.7.cloned.1.call-done = f32[2,32,4096]{2,1,0:T(8,128)} async-done(((f32[2,32,4096]{2,1,0:T(8,128)}), f32[2,32,4096]{2,1,0:T(8,128)}) %all-reduce.7.cloned.1.call-update) | async-done | bytes 1048592 | tf_op jit(solution)/shard_map/psum | solution.py:67
  613.9 362.4 %all-reduce.9.cloned.1.call-done = f32[2,32,4096]{2,1,0:T(8,128)} async-done(((f32[2,32,4096]{2,1,0:T(8,128)}), f32[2,32,4096]{2,1,0:T(8,128)}) %all-reduce.9.cloned.1.call-update) | async-done | bytes 1048592 | tf_op jit(solution)/shard_map/psum | solution.py:67
  (82 shorter events, 66.7 us)
Async XLA Ops:
  7.2 18.3 %copy-start = (f32[32,2,8,512]{3,2,1,0:T(8,128)S(1)}, f32[32,2,8,512]{3,2,1,0:T(8,128)}, u32[]{:S(2)}) copy-start(f32[32,2,8,512]{3,2,1,0:T(8,128)} %param.4) | copy-start | bytes 3145732
  7.2 606.1 %all-reduce.7.cloned.1.call-start = ((), (), s32[]{:S(2)}) async-start(), calls=%async_computation | async-start | bytes 2097152 | tf_op jit(solution)/shard_map/psum | solution.py:67
  9.1 16.2 %collective-permute-start = (f32[32,2,8,512]{3,0,2,1:T(8,128)S(1)}, f32[32,2,8,512]{3,0,2,1:T(8,128)S(1)}, u32[]{:S(2)}, u32[]{:S(2)}) collective-permute-start(f32[32,2,8,512]{3,0,2,1:T(8,128)S(1)} %copy.36), channel_id=1, source_target_pairs={{0,16},{16,32},{32,48},{48,64},{64,80},{80,96},{96,112},{112,128},... | collective-permute-start | bytes 3145736 | tf_op jit(solution)/shard_map/ppermute | solution.py:19
  13.7 16.4 %collective-permute-start.1 = (f32[32,2,8,512]{3,0,2,1:T(8,128)S(1)}, f32[32,2,8,512]{3,0,2,1:T(8,128)S(1)}, u32[]{:S(2)}, u32[]{:S(2)}) collective-permute-start(f32[32,2,8,512]{3,0,2,1:T(8,128)S(1)} %copy.36), channel_id=1, source_target_pairs={{16,0},{32,16},{48,32},{64,48},{80,64},{96,80},{112,96},{128,112},... | collective-permute-start | bytes 3145736 | tf_op jit(solution)/shard_map/ppermute | solution.py:20
  30.2 40.8 %copy-start.3 = (f32[2,8,512]{2,1,0:T(8,128)S(1)}, f32[2,8,512]{2,1,0:T(8,128)}, u32[]{:S(2)}) copy-start(f32[2,8,512]{2,1,0:T(8,128)} %param.5) | copy-start | bytes 98308
  30.3 12.5 %collective-permute-start.2 = (f32[32,6,2,512]{3,0,2,1:T(8,128)S(1)}, f32[32,6,2,512]{3,0,2,1:T(8,128)S(1)}, u32[]{:S(2)}, u32[]{:S(2)}) collective-permute-start(f32[32,6,2,512]{3,0,2,1:T(8,128)S(1)} %get-tuple-element.23), channel_id=1, source_target_pairs={{0,1},{1,2},{2,3},{3,4},{4,5},{5,6},{6,7},{7,8},{8,9},{9,10},{10,1... | collective-permute-start | bytes 2359304 | tf_op jit(solution)/shard_map/ppermute | solution.py:19
  33.9 37.1 %collective-permute-start.3 = (f32[32,6,2,512]{3,0,2,1:T(8,128)S(1)}, f32[32,6,2,512]{3,0,2,1:T(8,128)S(1)}, u32[]{:S(2)}, u32[]{:S(2)}) collective-permute-start(f32[32,6,2,512]{3,0,2,1:T(8,128)S(1)} %get-tuple-element.24), channel_id=1, source_target_pairs={{1,0},{2,1},{3,2},{4,3},{5,4},{6,5},{7,6},{8,7},{9,8},{10,9},{11,1... | collective-permute-start | bytes 2359304 | tf_op jit(solution)/shard_map/ppermute | solution.py:20
  72.6 14.4 %collective-permute-start.4 = (f32[32,2,8,512]{3,0,2,1:T(8,128)S(1)}, f32[32,2,8,512]{3,0,2,1:T(8,128)S(1)}, u32[]{:S(2)}, u32[]{:S(2)}) collective-permute-start(f32[32,2,8,512]{3,0,2,1:T(8,128)S(1)} %get-tuple-element.15), channel_id=1, source_target_pairs={{0,16},{16,32},{32,48},{48,64},{64,80},{80,96},{96,112},{112,128},... | collective-permute-start | bytes 3145736 | tf_op jit(solution)/shard_map/ppermute | solution.py:19
  75.3 16.1 %collective-permute-start.5 = (f32[32,2,8,512]{3,0,2,1:T(8,128)S(1)}, f32[32,2,8,512]{3,0,2,1:T(8,128)S(1)}, u32[]{:S(2)}, u32[]{:S(2)}) collective-permute-start(f32[32,2,8,512]{3,0,2,1:T(8,128)S(1)} %get-tuple-element.15), channel_id=1, source_target_pairs={{16,0},{32,16},{48,32},{64,48},{80,64},{96,80},{112,96},{128,112},... | collective-permute-start | bytes 3145736 | tf_op jit(solution)/shard_map/ppermute | solution.py:20
  91.6 16.7 %collective-permute-start.6 = (f32[32,6,2,512]{3,0,2,1:T(8,128)S(1)}, f32[32,6,2,512]{3,0,2,1:T(8,128)S(1)}, u32[]{:S(2)}, u32[]{:S(2)}) collective-permute-start(f32[32,6,2,512]{3,0,2,1:T(8,128)S(1)} %get-tuple-element.21), channel_id=1, source_target_pairs={{0,1},{1,2},{2,3},{3,4},{4,5},{5,6},{6,7},{7,8},{8,9},{9,10},{10,1... | collective-permute-start | bytes 2359304 | tf_op jit(solution)/shard_map/ppermute | solution.py:19
  99.4 35.2 %collective-permute-start.7 = (f32[32,6,2,512]{3,0,2,1:T(8,128)S(1)}, f32[32,6,2,512]{3,0,2,1:T(8,128)S(1)}, u32[]{:S(2)}, u32[]{:S(2)}) collective-permute-start(f32[32,6,2,512]{3,0,2,1:T(8,128)S(1)} %get-tuple-element.22), channel_id=1, source_target_pairs={{1,0},{2,1},{3,2},{4,3},{5,4},{6,5},{7,6},{8,7},{9,8},{10,9},{11,1... | collective-permute-start | bytes 2359304 | tf_op jit(solution)/shard_map/ppermute | solution.py:20
  136.9 13.7 %collective-permute-start.8 = (f32[32,2,8,512]{3,0,2,1:T(8,128)S(1)}, f32[32,2,8,512]{3,0,2,1:T(8,128)S(1)}, u32[]{:S(2)}, u32[]{:S(2)}) collective-permute-start(f32[32,2,8,512]{3,0,2,1:T(8,128)S(1)} %fusion.21), channel_id=1, source_target_pairs={{0,16},{16,32},{32,48},{48,64},{64,80},{80,96},{96,112},{112,128},... | collective-permute-start | bytes 3145736 | tf_op jit(solution)/shard_map/ppermute | solution.py:19
  138.9 16.1 %collective-permute-start.9 = (f32[32,2,8,512]{3,0,2,1:T(8,128)S(1)}, f32[32,2,8,512]{3,0,2,1:T(8,128)S(1)}, u32[]{:S(2)}, u32[]{:S(2)}) collective-permute-start(f32[32,2,8,512]{3,0,2,1:T(8,128)S(1)} %fusion.21), channel_id=1, source_target_pairs={{16,0},{32,16},{48,32},{64,48},{80,64},{96,80},{112,96},{128,112},... | collective-permute-start | bytes 3145736 | tf_op jit(solution)/shard_map/ppermute | solution.py:20
  155.1 11.9 %collective-permute-start.10 = (f32[32,6,2,512]{3,0,2,1:T(8,128)S(1)}, f32[32,6,2,512]{3,0,2,1:T(8,128)S(1)}, u32[]{:S(2)}, u32[]{:S(2)}) collective-permute-start(f32[32,6,2,512]{3,0,2,1:T(8,128)S(1)} %get-tuple-element.19), channel_id=1, source_target_pairs={{0,1},{1,2},{2,3},{3,4},{4,5},{5,6},{6,7},{7,8},{8,9},{9,10},{10,1... | collective-permute-start | bytes 2359304 | tf_op jit(solution)/shard_map/ppermute | solution.py:19
  158.1 39.4 %copy-start.5 = (s32[2,8,512]{2,1,0:T(8,128)S(1)}, s32[2,8,512]{2,1,0:T(8,128)}, u32[]{:S(2)}) copy-start(s32[2,8,512]{2,1,0:T(8,128)} %param.6) | copy-start | bytes 98308
  158.2 39.5 %slice-start = ((s32[1,1,8192]{2,1,0:T(1,128)}), s32[1,1,4096]{2,1,0:T(1,128)S(1)}, s32[]{:S(2)}) async-start(s32[1,1,8192]{2,1,0:T(1,128)} %param.7), calls=%async_computation.2 | async-start | bytes 32768 | tf_op jit(solution)/shard_map/slice | solution.py:63
  158.2 33.2 %collective-permute-start.11 = (f32[32,6,2,512]{3,0,2,1:T(8,128)S(1)}, f32[32,6,2,512]{3,0,2,1:T(8,128)S(1)}, u32[]{:S(2)}, u32[]{:S(2)}) collective-permute-start(f32[32,6,2,512]{3,0,2,1:T(8,128)S(1)} %get-tuple-element.20), channel_id=1, source_target_pairs={{1,0},{2,1},{3,2},{4,3},{5,4},{6,5},{7,6},{8,7},{9,8},{10,9},{11,1... | collective-permute-start | bytes 2359304 | tf_op jit(solution)/shard_map/ppermute | solution.py:20
  193.2 13.7 %collective-permute-start.12 = (f32[32,2,8,512]{3,0,2,1:T(8,128)S(1)}, f32[32,2,8,512]{3,0,2,1:T(8,128)S(1)}, u32[]{:S(2)}, u32[]{:S(2)}) collective-permute-start(f32[32,2,8,512]{3,0,2,1:T(8,128)S(1)} %fusion.32), channel_id=1, source_target_pairs={{0,16},{16,32},{32,48},{48,64},{64,80},{80,96},{96,112},{112,128},... | collective-permute-start | bytes 3145736 | tf_op jit(solution)/shard_map/ppermute | solution.py:19
  195.1 33.7 %collective-permute-start.13 = (f32[32,2,8,512]{3,0,2,1:T(8,128)S(1)}, f32[32,2,8,512]{3,0,2,1:T(8,128)S(1)}, u32[]{:S(2)}, u32[]{:S(2)}) collective-permute-start(f32[32,2,8,512]{3,0,2,1:T(8,128)S(1)} %fusion.32), channel_id=1, source_target_pairs={{16,0},{32,16},{48,32},{64,48},{80,64},{96,80},{112,96},{128,112},... | collective-permute-start | bytes 3145736 | tf_op jit(solution)/shard_map/ppermute | solution.py:20
  197.7 37.5 %copy-start.4 = (s32[1,1,8192]{2,1,0:T(1,128)S(1)}, s32[1,1,8192]{2,1,0:T(1,128)}, u32[]{:S(2)}) copy-start(s32[1,1,8192]{2,1,0:T(1,128)} %param.7) | copy-start | bytes 98308
  206.8 23.4 %copy-start.1 = (f32[32,2,8,512]{3,0,2,1:T(8,128)}, f32[32,2,8,512]{3,0,2,1:T(8,128)S(1)}, u32[]{:S(2)}) copy-start(f32[32,2,8,512]{3,0,2,1:T(8,128)S(1)} %collective-permute-done.12) | copy-start | bytes 3145732
  230.3 11.8 %collective-permute-start.14 = (f32[32,6,2,512]{3,0,2,1:T(8,128)}, f32[32,6,2,512]{3,0,2,1:T(8,128)}, u32[]{:S(2)}, u32[]{:S(2)}) collective-permute-start(f32[32,6,2,512]{3,0,2,1:T(8,128)} %get-tuple-element.17), channel_id=1, source_target_pairs={{0,1},{1,2},{2,3},{3,4},{4,5},{5,6},{6,7},{7,8},{8,9},{9,10},{10,1... | collective-permute-start | bytes 2359304 | tf_op jit(solution)/shard_map/ppermute | solution.py:19
  233.7 36.1 %collective-permute-start.15 = (f32[32,6,2,512]{3,0,2,1:T(8,128)}, f32[32,6,2,512]{3,0,2,1:T(8,128)}, u32[]{:S(2)}, u32[]{:S(2)}) collective-permute-start(f32[32,6,2,512]{3,0,2,1:T(8,128)} %get-tuple-element.18), channel_id=1, source_target_pairs={{1,0},{2,1},{3,2},{4,3},{5,4},{6,5},{7,6},{8,7},{9,8},{10,9},{11,1... | collective-permute-start | bytes 2359304 | tf_op jit(solution)/shard_map/ppermute | solution.py:20
  299.6 676.8 %all-reduce.9.cloned.1.call-start = ((), (), s32[]{:S(2)}) async-start(), calls=%async_computation.1 | async-start | bytes 2097152 | tf_op jit(solution)/shard_map/psum | solution.py:67
  (1 other events, 1.5 us)
Sparse Core Ops, SparseCore 0:
  299.7 313.4 all-reduce.6
  616.4 359.8 all-reduce.8
